TPU v7x, 128 devices: a whole 4x4x4 slice. The times are simulated.
128 devices in a mesh: hot: 4 (over z), dom: 32 (over y, x, core).
Axes of the slice: x: 4, y: 4, z: 4, core: 2. Of those that a mesh axis runs over, the one named last changes fastest.
Arguments:
- macro_adjoint: float32 [16, 6], P('hot'), may hold values from -6 to 6
- slip_code: int32 [32, 64, 4096], P('hot', 'dom'), may hold values from 0 to 4095
- grain_id: int32 [32, 64, 4096], P('hot', 'dom'), may hold values from 0 to 63
- grain_modulus: float32 [64], replicated, may hold values from 0.5 to 4
- slip_softening: float32 [64, 12], replicated, may hold values from 0.1 to 1.5
- rve_spot: int32 [32], P('hot'), may hold values from 0 to 15, as said below
Outputs:
- sensitivity: float32 [16, 6], P('hot')
- adjoint_field: float32 [32, 3, 64, 4096], P('hot', None, 'dom')
Inputs may be any that keep to these rules, and one draw needn't show every extreme that they name: `rve_spot`: every hot-spot is named by exactly 2 RVEs.
All inputs are finite; a program needn't handle non-finite values.
Results may differ from a plain program's by a relative error of at most 0.0003.
Values sent between devices are 32-bit elements; how exact they have to be, the bound alone decides.
No kernel may reach another device: no remote copies, remote signals or barrier semaphores. Data moves between devices by JAX's collectives and lax.ppermute only.
A program may use at most 64 MiB of HBM per device.

v0:
```python
import jax
import jax.numpy as jnp
from jax import lax
from jax.sharding import PartitionSpec as P

RES = 64
SLIPS = 12
GRAINS = 64
ITERS = 8
mass_term = 0.02


def padded_2(value, sides, width):
    for axis, dim in sides:
        devices, length = (lax.axis_size(axis), value.shape[dim])
        up = [(i, (i + 1) % devices) for i in range(devices - 1)]
        down = [(j, i) for i, j in up]
        last = lax.slice_in_dim(value, length - width, length, axis=dim)
        leading = lax.slice_in_dim(value, 0, width, axis=dim)
        before = lax.ppermute(last, axis, up)
        after = lax.ppermute(leading, axis, down)
        value = jnp.concatenate([before, value, after], axis=dim)
    return value


def shift_cells(field, step):
    filler = jnp.zeros(field.shape[:-1] + (abs(step),), field.dtype)
    if step > 0:
        return jnp.concatenate([field[..., step:], filler], -1)
    return jnp.concatenate([filler, field[..., :step]], -1)


def local_dot(first, second):
    return jnp.sum(first * second, axis=(1, 2, 3))


def shards(macro_adjoint, slip_code, grain_id, grain_modulus, slip_softening, rve_spot):
    rve_count = slip_code.shape[0]
    cells = slip_code.shape[2]
    spot_count = macro_adjoint.shape[0] * lax.axis_size("hot")
    column = jnp.arange(cells) % RES
    upper_mask = (column != RES - 1).astype(jnp.float32)
    lower_mask = (column != 0).astype(jnp.float32)
    table = jnp.concatenate([grain_modulus[None, :], slip_softening.T], 0)

    def stiff_one(inputs):
        codes, grain_cells = inputs
        flat_codes = codes.reshape(-1)
        flat_grains = grain_cells.reshape(-1)
        onehot = (jnp.arange(GRAINS)[:, None] == flat_grains[None, :]).astype(jnp.float32)
        looked = jnp.dot(
            table, onehot, precision=lax.Precision.HIGHEST, preferred_element_type=jnp.float32
        )
        softening = jnp.zeros(flat_codes.shape, jnp.float32)
        for slip in range(SLIPS):
            active = (flat_codes // 2**slip % 2).astype(jnp.float32)
            softening = softening + active * looked[1 + slip]
        return (looked[0] / (1.0 + softening)).reshape(codes.shape)

    all_strains = lax.all_gather(macro_adjoint, "hot", axis=0, tiled=True)
    spot_onehot = (rve_spot[:, None] == jnp.arange(spot_count)[None, :]).astype(jnp.float32)
    strains = jnp.dot(
        spot_onehot,
        all_strains,
        precision=lax.Precision.HIGHEST,
        preferred_element_type=jnp.float32,
    )
    stiff = lax.map(stiff_one, (slip_code, grain_id))
    padded = padded_2(stiff, (("dom", 1),), 1)

    def squares(residual):
        return lax.psum(local_dot(residual, residual), "dom")

    near_xup = padded[:, 2:]
    near_xdn = padded[:, :-2]
    near_yup = shift_cells(stiff, RES)
    near_ydn = shift_cells(stiff, -RES)
    near_zup = shift_cells(stiff, 1) * upper_mask
    near_zdn = shift_cells(stiff, -1) * lower_mask
    face_xup = 0.5 * (stiff + near_xup)
    face_xdn = 0.5 * (stiff + near_xdn)
    face_yup = 0.5 * (stiff + near_yup)
    face_ydn = 0.5 * (stiff + near_ydn)
    face_zup = 0.5 * (stiff + near_zup)
    face_zdn = 0.5 * (stiff + near_zdn)
    diagonal_sum = (mass_term + face_xup + face_xdn + face_yup + face_ydn + face_zup + face_zdn)[
        :, None
    ]
    gradients = [
        0.5 * (near_xup - near_xdn),
        0.5 * (near_yup - near_ydn),
        0.5 * (near_zup - near_zdn),
    ]
    tensor = [
        [strains[:, 0], strains[:, 5], strains[:, 4]],
        [strains[:, 5], strains[:, 1], strains[:, 3]],
        [strains[:, 4], strains[:, 3], strains[:, 2]],
    ]
    source = jnp.stack(
        [
            gradients[0] * tensor[comp][0][:, None, None]
            + gradients[1] * tensor[comp][1][:, None, None]
            + gradients[2] * tensor[comp][2][:, None, None]
            for comp in range(3)
        ],
        1,
    )

    def expand(values):
        return values[:, None, None, None]

    answer = jnp.zeros_like(source)
    residual = source
    direction = source
    norm_now = squares(residual)
    for step in range(ITERS):
        wide = padded_2(direction, (("dom", 2),), 1)
        image = (
            diagonal_sum * direction
            - face_xup[:, None] * wide[:, :, 2:]
            - face_xdn[:, None] * wide[:, :, :-2]
            - face_yup[:, None] * shift_cells(direction, RES)
            - face_ydn[:, None] * shift_cells(direction, -RES)
            - face_zup[:, None] * (shift_cells(direction, 1) * upper_mask)
            - face_zdn[:, None] * (shift_cells(direction, -1) * lower_mask)
        )
        alpha = norm_now / lax.psum(local_dot(direction, image), "dom")
        answer = answer + expand(alpha) * direction
        residual = residual - expand(alpha) * image
        norm_next = squares(residual)
        direction = residual + expand(norm_next / norm_now) * direction
        norm_now = norm_next
    volume = float(RES**3)
    stiff_part = jnp.sum(stiff, axis=(1, 2)) / volume
    moment = [
        [jnp.sum(answer[:, comp] * gradients[other], axis=(1, 2)) for other in range(3)]
        for comp in range(3)
    ]
    pairs = [(0, 0), (1, 1), (2, 2), (1, 2), (0, 2), (0, 1)]
    partial_here = jnp.stack(
        [
            stiff_part * strains[:, slot]
            - 0.5
            * (moment[pairs[slot][0]][pairs[slot][1]] + moment[pairs[slot][1]][pairs[slot][0]])
            / volume
            for slot in range(6)
        ],
        1,
    )
    per_spot = float(rve_count * lax.axis_size("hot") // spot_count)
    rve_totals = lax.psum(partial_here, "dom")
    spot_local = jnp.dot(
        spot_onehot.T,
        rve_totals,
        precision=lax.Precision.HIGHEST,
        preferred_element_type=jnp.float32,
    )
    owned = lax.psum_scatter(spot_local, "hot", scatter_dimension=0, tiled=True)
    return (owned / per_spot, answer)


def solution(mesh):
    return jax.shard_map(
        shards,
        mesh=mesh,
        in_specs=(P("hot", None), P("hot", "dom", None), P("hot", "dom", None), P(), P(), P("hot")),
        out_specs=(P("hot", None), P("hot", None, "dom", None)),
        check_vma=False,
    )
```

profile of v0, /device:TPU:0, one launch (start us, length us, event | category | flops | bytes accessed | tf_op | source)
XLA Modules:
  0.0 1254.9 jit_solution(1973612798460784764)
XLA Ops:
  1.3 40.5 %while.13 = (s32[]{:T(128)}, f32[8,2,4096]{2,1,0:T(2,128)S(1)}, s32[8,2,4096]{2,1,0:T(2,128)}, f32[13,64]{1,0:T(8,128)S(1)}, s32[8,2,4096]{2,1,0:T(2,128)}, /*index=5*/s32[]{:T(128)}) while((s32[]{:T(128)}, f32[8,2,4096]{2,1,0:T(2,128)S(1)}, s32[8,2,4096]{2,1,0:T(2,128)}, f32[13,64]{1,0:T(8,128)S(1)}, s32[8,2,4096]{2,1,0:T(2,128)}, ...), condition=%wide.region_1.2_spmd, body=%wide.region_0.1_spmd.sunk | while | flops 84582400 | bytes 2788685 | solution.py:68
  4.3 2.1 divide_dynamic-update-slice_fusion.2
  9.4 2.1 divide_dynamic-update-slice_fusion.2
  14.4 2.1 divide_dynamic-update-slice_fusion.2
  19.5 2.1 divide_dynamic-update-slice_fusion.2
  43.4 3.0 collective-permute-start.1
  47.5 12.1 all-gather
  66.5 3.2 collective-permute-start.3
  71.3 5.7 multiply_reduce_fusion.14
  77.0 67.4 %all-reduce.37 = (f32[8]{0:T(128)S(1)}, f32[8]{0:T(128)S(1)}) all-reduce(f32[8]{0:T(128)S(1)} %get-tuple-element.148, f32[8]{0:T(128)S(1)} %get-tuple-element.147), channel_id=1, replica_groups=mesh['hot'=4,'dom'=32] {'dom'}, use_global_device_ids=true, to_apply=%region_4.5 | all-reduce | flops 16 | bytes 128 | tf_op jit(solution)/shard_map/psum | solution.py:72
  146.3 62.9 %psum.121 = f32[8]{0:T(128)S(1)} all-reduce(f32[8]{0:T(128)S(1)} %get-tuple-element.185), channel_id=1, replica_groups=mesh['hot'=4,'dom'=32] {'dom'}, use_global_device_ids=true, to_apply=%region_8.9 | all-reduce | flops 8 | bytes 64 | tf_op jit(solution)/shard_map/psum | solution.py:72
  214.1 3.1 collective-permute-start.5
  218.4 5.4 multiply_reduce_fusion.12
  223.8 66.8 %psum.122 = f32[8]{0:T(128)S(1)} all-reduce(f32[8]{0:T(128)S(1)} %get-tuple-element.183), channel_id=1, replica_groups=mesh['hot'=4,'dom'=32] {'dom'}, use_global_device_ids=true, to_apply=%region_10.11 | all-reduce | flops 8 | bytes 64 | tf_op jit(solution)/shard_map/psum | solution.py:127
  290.7 2.7 multiply_reduce_fusion.11
  293.4 62.7 %psum.123 = f32[8]{0:T(128)S(1)} all-reduce(f32[8]{0:T(128)S(1)} %get-tuple-element.181), channel_id=1, replica_groups=mesh['hot'=4,'dom'=32] {'dom'}, use_global_device_ids=true, to_apply=%region_12.13 | all-reduce | flops 8 | bytes 64 | tf_op jit(solution)/shard_map/psum | solution.py:72
  356.0 2.3 multiply_add_fusion.6
  361.4 3.3 collective-permute-start.7
  365.8 5.4 multiply_reduce_fusion.10
  371.2 67.1 %psum.124 = f32[8]{0:T(128)S(1)} all-reduce(f32[8]{0:T(128)S(1)} %get-tuple-element.179), channel_id=1, replica_groups=mesh['hot'=4,'dom'=32] {'dom'}, use_global_device_ids=true, to_apply=%region_14.15 | all-reduce | flops 8 | bytes 64 | tf_op jit(solution)/shard_map/psum | solution.py:127
  438.3 2.6 multiply_reduce_fusion.9
  440.9 62.7 %psum.125 = f32[8]{0:T(128)S(1)} all-reduce(f32[8]{0:T(128)S(1)} %get-tuple-element.177), channel_id=1, replica_groups=mesh['hot'=4,'dom'=32] {'dom'}, use_global_device_ids=true, to_apply=%region_16.17 | all-reduce | flops 8 | bytes 64 | tf_op jit(solution)/shard_map/psum | solution.py:72
  508.3 3.1 collective-permute-start.9
  512.6 5.4 multiply_reduce_fusion.8
  518.1 67.1 %psum.126 = f32[8]{0:T(128)S(1)} all-reduce(f32[8]{0:T(128)S(1)} %get-tuple-element.175), channel_id=1, replica_groups=mesh['hot'=4,'dom'=32] {'dom'}, use_global_device_ids=true, to_apply=%region_18.19 | all-reduce | flops 8 | bytes 64 | tf_op jit(solution)/shard_map/psum | solution.py:127
  585.2 2.8 multiply_reduce_fusion.7
  588.0 62.7 %psum.127 = f32[8]{0:T(128)S(1)} all-reduce(f32[8]{0:T(128)S(1)} %get-tuple-element.173), channel_id=1, replica_groups=mesh['hot'=4,'dom'=32] {'dom'}, use_global_device_ids=true, to_apply=%region_20.21 | all-reduce | flops 8 | bytes 64 | tf_op jit(solution)/shard_map/psum | solution.py:72
  655.4 3.6 collective-permute-start.11
  660.0 5.5 multiply_reduce_fusion.6
  665.5 67.1 %psum.128 = f32[8]{0:T(128)S(1)} all-reduce(f32[8]{0:T(128)S(1)} %get-tuple-element.171), channel_id=1, replica_groups=mesh['hot'=4,'dom'=32] {'dom'}, use_global_device_ids=true, to_apply=%region_22.23 | all-reduce | flops 8 | bytes 64 | tf_op jit(solution)/shard_map/psum | solution.py:127
  732.6 2.8 multiply_reduce_fusion.5
  735.4 62.7 %psum.129 = f32[8]{0:T(128)S(1)} all-reduce(f32[8]{0:T(128)S(1)} %get-tuple-element.169), channel_id=1, replica_groups=mesh['hot'=4,'dom'=32] {'dom'}, use_global_device_ids=true, to_apply=%region_24.25 | all-reduce | flops 8 | bytes 64 | tf_op jit(solution)/shard_map/psum | solution.py:72
  802.8 3.2 collective-permute-start.13
  807.4 5.5 multiply_reduce_fusion.4
  812.9 67.1 %psum.130 = f32[8]{0:T(128)S(1)} all-reduce(f32[8]{0:T(128)S(1)} %get-tuple-element.167), channel_id=1, replica_groups=mesh['hot'=4,'dom'=32] {'dom'}, use_global_device_ids=true, to_apply=%region_26.27 | all-reduce | flops 8 | bytes 64 | tf_op jit(solution)/shard_map/psum | solution.py:127
  880.0 2.8 multiply_reduce_fusion.3
  882.8 62.7 %psum.131 = f32[8]{0:T(128)S(1)} all-reduce(f32[8]{0:T(128)S(1)} %get-tuple-element.165), channel_id=1, replica_groups=mesh['hot'=4,'dom'=32] {'dom'}, use_global_device_ids=true, to_apply=%region_28.29 | all-reduce | flops 8 | bytes 64 | tf_op jit(solution)/shard_map/psum | solution.py:72
  950.3 3.4 collective-permute-start.15
  954.8 5.5 multiply_reduce_fusion.2
  960.4 67.1 %psum.132 = f32[8]{0:T(128)S(1)} all-reduce(f32[8]{0:T(128)S(1)} %get-tuple-element.163), channel_id=1, replica_groups=mesh['hot'=4,'dom'=32] {'dom'}, use_global_device_ids=true, to_apply=%region_30.31 | all-reduce | flops 8 | bytes 64 | tf_op jit(solution)/shard_map/psum | solution.py:127
  1027.5 2.8 multiply_reduce_fusion.1
  1030.3 62.7 %psum.133 = f32[8]{0:T(128)S(1)} all-reduce(f32[8]{0:T(128)S(1)} %get-tuple-element.161), channel_id=1, replica_groups=mesh['hot'=4,'dom'=32] {'dom'}, use_global_device_ids=true, to_apply=%region_32.33 | all-reduce | flops 8 | bytes 64 | tf_op jit(solution)/shard_map/psum | solution.py:72
  1093.0 5.2 multiply_add_fusion.1
  1101.3 3.2 collective-permute-start.17
  1105.8 4.3 multiply_reduce_fusion
  1110.7 67.1 %psum.134 = f32[8]{0:T(128)S(1)} all-reduce(f32[8]{0:T(128)S(1)} %multiply_reduce_fusion), channel_id=1, replica_groups=mesh['hot'=4,'dom'=32] {'dom'}, use_global_device_ids=true, to_apply=%region_34.35 | all-reduce | flops 8 | bytes 64 | tf_op jit(solution)/shard_map/psum | solution.py:127
  1181.1 62.7 %psum.135 = f32[8,6]{0,1:T(8,128)S(1)} all-reduce(f32[8,6]{0,1:T(8,128)S(1)} %stack.25), channel_id=1, replica_groups=mesh['hot'=4,'dom'=32] {'dom'}, use_global_device_ids=true, to_apply=%region_44.45 | all-reduce | flops 48 | bytes 384 | tf_op jit(solution)/shard_map/psum | solution.py:151
  1244.1 10.0 all-reduce.36
  (351 shorter events, 86.8 us)
Async XLA Ops:
  42.1 18.4 %collective-permute-start = (f32[8,1,4096]{2,1,0:T(1,128)S(1)}, f32[8,1,4096]{2,1,0:T(1,128)S(1)}, u32[]{:S(2)}, u32[]{:S(2)}) collective-permute-start(f32[8,1,4096]{2,1,0:T(1,128)S(1)} %get-tuple-element.256), channel_id=1, source_target_pairs={{1,0},{2,1},{3,2},{4,3},{5,4},{6,5},{7,6},{8,7},{9,8},{10,9},{11,1... | collective-permute-start | bytes 393224 | tf_op jit(solution)/shard_map/ppermute | solution.py:21
  43.4 17.1 %collective-permute-start.1 = (f32[8,1,4096]{2,1,0:T(1,128)S(1)}, f32[8,1,4096]{2,1,0:T(1,128)S(1)}, u32[]{:S(2)}, u32[]{:S(2)}) collective-permute-start(f32[8,1,4096]{2,1,0:T(1,128)S(1)} %get-tuple-element.257), channel_id=1, source_target_pairs={{0,1},{1,2},{2,3},{3,4},{4,5},{5,6},{6,7},{7,8},{8,9},{9,10},{10,1... | collective-permute-start | bytes 393224 | tf_op jit(solution)/shard_map/ppermute | solution.py:20
  46.7 14.8 %copy-start.45 = (f32[8,2,4095]{2,1,0:T(2,128)}, f32[8,2,4095]{2,1,0:T(2,128)S(1)}, u32[]{:S(2)}) copy-start(f32[8,2,4095]{2,1,0:T(2,128)S(1)} %get-tuple-element.252) | copy-start | bytes 786244
  46.8 14.8 %copy-start.47 = (f32[8,2,4095]{2,1,0:T(2,128)}, f32[8,2,4095]{2,1,0:T(2,128)S(1)}, u32[]{:S(2)}) copy-start(f32[8,2,4095]{2,1,0:T(2,128)S(1)} %get-tuple-element.253) | copy-start | bytes 786244
  46.8 12.8 %copy-start.58 = (s32[8]{0:T(128)S(1)}, s32[8]{0:T(128)}, u32[]{:S(2)}) copy-start(s32[8]{0:T(128)} %param.13) | copy-start | bytes 100
  46.8 13.0 %copy-start.59 = (u32[128]{0:T(128)S(1)}, u32[128]{0:T(128)}, u32[]{:S(2)}) copy-start(u32[128]{0:T(128)} %constant.499) | copy-start | bytes 1540
  47.1 14.4 %copy-start.49 = (f32[8,2,4032]{2,1,0:T(2,128)}, f32[8,2,4032]{2,1,0:T(2,128)S(1)}, u32[]{:S(2)}) copy-start(f32[8,2,4032]{2,1,0:T(2,128)S(1)} %get-tuple-element.254) | copy-start | bytes 774148
  47.1 14.4 %copy-start.51 = (f32[8,2,4032]{2,1,0:T(2,128)}, f32[8,2,4032]{2,1,0:T(2,128)S(1)}, u32[]{:S(2)}) copy-start(f32[8,2,4032]{2,1,0:T(2,128)S(1)} %get-tuple-element.255) | copy-start | bytes 774148
  61.6 82.8 %copy-start.30 = (f32[8,1,2,4096]{3,2,0,1:T(2,128)}, f32[8,1,2,4096]{3,2,0,1:T(2,128)S(1)}, u32[]{:S(2)}) copy-start(f32[8,1,2,4096]{3,2,0,1:T(2,128)S(1)} %get-tuple-element.195) | copy-start | bytes 786436
  62.1 82.4 %copy-start.32 = (f32[8,1,2,4096]{3,2,0,1:T(2,128)}, f32[8,1,2,4096]{3,2,0,1:T(2,128)S(1)}, u32[]{:S(2)}) copy-start(f32[8,1,2,4096]{3,2,0,1:T(2,128)S(1)} %get-tuple-element.199) | copy-start | bytes 786436
  62.1 82.3 %copy-start.34 = (f32[8,1,2,4096]{3,2,0,1:T(2,128)}, f32[8,1,2,4096]{3,2,0,1:T(2,128)S(1)}, u32[]{:S(2)}) copy-start(f32[8,1,2,4096]{3,2,0,1:T(2,128)S(1)} %get-tuple-element.200) | copy-start | bytes 786436
  64.3 5.5 copy-start.46
  64.3 5.5 copy-start.48
  64.3 5.5 copy-start.50
  64.3 5.5 copy-start.52
  64.3 5.5 copy-start.54
  64.4 5.5 copy-start.56
  65.2 6.0 collective-permute-start.2
  66.5 4.7 collective-permute-start.3
  71.2 441.4 %copy-start.14 = (f32[8,2,4096]{2,1,0:T(2,128)}, f32[8,2,4096]{2,1,0:T(2,128)S(1)}, u32[]{:S(2)}) copy-start(f32[8,2,4096]{2,1,0:T(2,128)S(1)} %get-tuple-element.192) | copy-start | bytes 786436
  71.2 441.4 %copy-start.19 = (f32[8,2,4096]{2,1,0:T(2,128)}, f32[8,2,4096]{2,1,0:T(2,128)S(1)}, u32[]{:S(2)}) copy-start(f32[8,2,4096]{2,1,0:T(2,128)S(1)} %get-tuple-element.193) | copy-start | bytes 786436
  71.2 441.4 %copy-start.24 = (f32[8,2,4096]{2,1,0:T(2,128)}, f32[8,2,4096]{2,1,0:T(2,128)S(1)}, u32[]{:S(2)}) copy-start(f32[8,2,4096]{2,1,0:T(2,128)S(1)} %get-tuple-element.194) | copy-start | bytes 786436
  71.2 588.7 %copy-start.2 = (f32[8,2,4096]{2,1,0:T(2,128)}, f32[8,2,4096]{2,1,0:T(2,128)S(1)}, u32[]{:S(2)}) copy-start(f32[8,2,4096]{2,1,0:T(2,128)S(1)} %get-tuple-element.189) | copy-start | bytes 786436
  71.2 588.7 %copy-start.6 = (f32[8,2,4096]{2,1,0:T(2,128)}, f32[8,2,4096]{2,1,0:T(2,128)S(1)}, u32[]{:S(2)}) copy-start(f32[8,2,4096]{2,1,0:T(2,128)S(1)} %get-tuple-element.190) | copy-start | bytes 786436
  71.2 588.7 %copy-start.10 = (f32[8,2,4096]{2,1,0:T(2,128)}, f32[8,2,4096]{2,1,0:T(2,128)S(1)}, u32[]{:S(2)}) copy-start(f32[8,2,4096]{2,1,0:T(2,128)S(1)} %get-tuple-element.191) | copy-start | bytes 786436
  146.3 144.3 %copy-start.29 = (f32[8,3,2,4096]{3,2,0,1:T(2,128)}, f32[8,3,2,4096]{3,2,0,1:T(2,128)S(1)}, u32[]{:S(2)}) copy-start(f32[8,3,2,4096]{3,2,0,1:T(2,128)S(1)} %get-tuple-element.186) | copy-start | bytes 2359300
  212.8 5.3 collective-permute-start.4
  214.1 4.4 collective-permute-start.5
  290.7 65.3 %copy-start.31 = (f32[8,1,2,4096]{3,2,0,1:T(2,128)S(1)}, f32[8,1,2,4096]{3,2,0,1:T(2,128)}, u32[]{:S(2)}) copy-start(f32[8,1,2,4096]{3,2,0,1:T(2,128)} %copy-done.30) | copy-start | bytes 786436
  290.7 65.4 %copy-start.33 = (f32[8,1,2,4096]{3,2,0,1:T(2,128)S(1)}, f32[8,1,2,4096]{3,2,0,1:T(2,128)}, u32[]{:S(2)}) copy-start(f32[8,1,2,4096]{3,2,0,1:T(2,128)} %copy-done.32) | copy-start | bytes 786436
  290.7 65.3 %copy-start.35 = (f32[8,1,2,4096]{3,2,0,1:T(2,128)S(1)}, f32[8,1,2,4096]{3,2,0,1:T(2,128)}, u32[]{:S(2)}) copy-start(f32[8,1,2,4096]{3,2,0,1:T(2,128)} %copy-done.34) | copy-start | bytes 786436
  360.1 5.5 collective-permute-start.6
  361.4 4.4 collective-permute-start.7
  365.8 72.5 %copy-start.36 = (f32[8,3,2,4096]{3,2,0,1:T(2,128)S(1)}, f32[8,3,2,4096]{3,2,0,1:T(2,128)}, u32[]{:S(2)}) copy-start(f32[8,3,2,4096]{3,2,0,1:T(2,128)} %get-tuple-element.182) | copy-start | bytes 2359300
  507.0 5.3 collective-permute-start.8
  508.3 4.4 collective-permute-start.9
  654.1 5.8 collective-permute-start.10
  655.4 4.6 copy-start.15
  655.4 4.5 collective-permute-start.11
  801.5 5.5 collective-permute-start.12
  802.8 4.5 collective-permute-start.13
  947.1 7.6 copy-start.1
  948.9 5.6 collective-permute-start.14
  950.3 4.5 collective-permute-start.15
  1098.1 7.6 copy-start
  1099.9 5.5 collective-permute-start.16
  1101.3 4.5 collective-permute-start.17
  1105.8 72.1 %copy-start.37 = (f32[8,3,2,4096]{3,2,0,1:T(2,128)S(1)}, f32[8,3,2,4096]{3,2,0,1:T(2,128)}, u32[]{:S(2)}) copy-start(f32[8,3,2,4096]{3,2,0,1:T(2,128)} %get-tuple-element.201) | copy-start | bytes 2359300
  (30 other events, 103.4 us)
where the time goes:
time: 1260 us; the launch traced here: 1250 us
  blocking collectives  1060 us (84%)
  other arithmetic  101 us (8%)
  starting transfers between devices  40.6 us (3%)
  local copies, waits for them, and re-layouts  40.4 us (3%)
    psum x8, blocking collectives, squares(): return lax.psum(local_dot(residual, residual), 'dom')  506 us
    psum x7, blocking collectives, shards(): alpha = norm_now / lax.psum(local_dot(direction, image), 'dom')  470 us
    psum x1, blocking collectives, shards(): rve_totals = lax.psum(partial_here, 'dom')  62.7 us
    reduce_sum x15, other arithmetic, local_dot(): return jnp.sum(first * second, axis=(1, 2, 3))  61.2 us
    ppermute x9, starting transfers between devices, padded_2(): before = lax.ppermute(last, axis, up)  29 us
  transfers between devices with their start and end apart: 18, of which 6 were waited for; matrix products, arithmetic and copies ran while one was open for 1% of the time, Pallas kernels for 0%

commit v1 on v0

--- a/solution.py
+++ b/solution.py
@@ -148,7 +148,13 @@
         1,
     )
     per_spot = float(rve_count * lax.axis_size("hot") // spot_count)
-    rve_totals = lax.psum(partial_here, "dom")
+    size = lax.axis_size("dom")
+    rve_totals, hop = (partial_here, 1)
+    while hop < size:
+        rve_totals = rve_totals + lax.ppermute(
+            rve_totals, "dom", [(i_2, i_2 ^ hop) for i_2 in range(size)]
+        )
+        hop = 2 * hop
     spot_local = jnp.dot(
         spot_onehot.T,
         rve_totals,

time: 1260 us -> 1220 us (0.968)
  blocking collectives: 1060 us -> 998 us
  waiting for transfers between devices: 2.06 us -> 19.3 us
    psum x1 -> x0, blocking collectives: 62.7 us -> none  [shards(): rve_totals = lax.psum(partial_here, 'dom')]
    ppermute x0 -> x5, waiting for transfers between devices: none -> 17.3 us  [shards(): lax.ppermute(rve_totals, 'dom', [(i_2, i_2 ^ hop) for i_2 in range(size)])]
  transfers between devices with their start and end apart: 18 -> 23, of which waited for: 6 -> 11; matrix products, arithmetic and copies ran while one was open for 1% -> 1% of each run, Pallas kernels for 0% -> 0%
where the time goes in v1:
time: 1220 us; the launch traced here: 1210 us
  blocking collectives  998 us (82%)
  other arithmetic  102 us (8%)
  local copies, waits for them, and re-layouts  40.9 us (3%)
  starting transfers between devices  40.7 us (3%)
  waiting for transfers between devices  19.3 us (2%)
    psum x8, blocking collectives, squares(): return lax.psum(local_dot(residual, residual), 'dom')  506 us
    psum x7, blocking collectives, shards(): alpha = norm_now / lax.psum(local_dot(direction, image), 'dom')  469 us
    reduce_sum x15, other arithmetic, local_dot(): return jnp.sum(first * second, axis=(1, 2, 3))  61.2 us
    ppermute x9, starting transfers between devices, padded_2(): before = lax.ppermute(last, axis, up)  29 us
  transfers between devices with their start and end apart: 23, of which 11 were waited for; matrix products, arithmetic and copies ran while one was open for 1% of the time, Pallas kernels for 0%

profile of v1, /device:TPU:0, one launch (start us, length us, event | category | flops | bytes accessed | tf_op | source)
XLA Modules:
  0.0 1211.1 jit_solution(14328796265763914335)
XLA Ops:
  1.3 40.5 %while.13 = (s32[]{:T(128)}, f32[8,2,4096]{2,1,0:T(2,128)S(1)}, s32[8,2,4096]{2,1,0:T(2,128)}, f32[13,64]{1,0:T(8,128)S(1)}, s32[8,2,4096]{2,1,0:T(2,128)}, /*index=5*/s32[]{:T(128)}) while((s32[]{:T(128)}, f32[8,2,4096]{2,1,0:T(2,128)S(1)}, s32[8,2,4096]{2,1,0:T(2,128)}, f32[13,64]{1,0:T(8,128)S(1)}, s32[8,2,4096]{2,1,0:T(2,128)}, ...), condition=%wide.region_1.2_spmd, body=%wide.region_0.1_spmd.sunk | while | flops 84582400 | bytes 2788685 | solution.py:68
  4.3 2.1 divide_dynamic-update-slice_fusion.2
  43.4 3.0 collective-permute-start.1
  47.4 12.1 all-gather
  66.4 3.2 collective-permute-start.3
  71.0 5.7 multiply_reduce_fusion.14
  76.7 67.5 %all-reduce.37 = (f32[8]{0:T(128)S(1)}, f32[8]{0:T(128)S(1)}) all-reduce(f32[8]{0:T(128)S(1)} %get-tuple-element.148, f32[8]{0:T(128)S(1)} %get-tuple-element.147), channel_id=1, replica_groups=mesh['hot'=4,'dom'=32] {'dom'}, use_global_device_ids=true, to_apply=%region_4.5 | all-reduce | flops 16 | bytes 128 | tf_op jit(solution)/shard_map/psum | solution.py:72
  146.3 62.9 %psum.114 = f32[8]{0:T(128)S(1)} all-reduce(f32[8]{0:T(128)S(1)} %get-tuple-element.185), channel_id=1, replica_groups=mesh['hot'=4,'dom'=32] {'dom'}, use_global_device_ids=true, to_apply=%region_8.9 | all-reduce | flops 8 | bytes 64 | tf_op jit(solution)/shard_map/psum | solution.py:72
  214.2 3.1 collective-permute-start.5
  218.6 5.4 multiply_reduce_fusion.12
  224.0 66.8 %psum.115 = f32[8]{0:T(128)S(1)} all-reduce(f32[8]{0:T(128)S(1)} %get-tuple-element.183), channel_id=1, replica_groups=mesh['hot'=4,'dom'=32] {'dom'}, use_global_device_ids=true, to_apply=%region_10.11 | all-reduce | flops 8 | bytes 64 | tf_op jit(solution)/shard_map/psum | solution.py:127
  290.8 2.6 multiply_reduce_fusion.11
  293.4 62.7 %psum.116 = f32[8]{0:T(128)S(1)} all-reduce(f32[8]{0:T(128)S(1)} %get-tuple-element.181), channel_id=1, replica_groups=mesh['hot'=4,'dom'=32] {'dom'}, use_global_device_ids=true, to_apply=%region_12.13 | all-reduce | flops 8 | bytes 64 | tf_op jit(solution)/shard_map/psum | solution.py:72
  356.1 2.5 multiply_add_fusion.6
  361.6 3.3 collective-permute-start.7
  366.0 5.4 multiply_reduce_fusion.10
  371.4 67.1 %psum.117 = f32[8]{0:T(128)S(1)} all-reduce(f32[8]{0:T(128)S(1)} %get-tuple-element.179), channel_id=1, replica_groups=mesh['hot'=4,'dom'=32] {'dom'}, use_global_device_ids=true, to_apply=%region_14.15 | all-reduce | flops 8 | bytes 64 | tf_op jit(solution)/shard_map/psum | solution.py:127
  438.5 2.6 multiply_reduce_fusion.9
  441.1 62.7 %psum.118 = f32[8]{0:T(128)S(1)} all-reduce(f32[8]{0:T(128)S(1)} %get-tuple-element.177), channel_id=1, replica_groups=mesh['hot'=4,'dom'=32] {'dom'}, use_global_device_ids=true, to_apply=%region_16.17 | all-reduce | flops 8 | bytes 64 | tf_op jit(solution)/shard_map/psum | solution.py:72
  508.6 3.1 collective-permute-start.9
  513.0 5.4 multiply_reduce_fusion.8
  518.5 67.1 %psum.119 = f32[8]{0:T(128)S(1)} all-reduce(f32[8]{0:T(128)S(1)} %get-tuple-element.175), channel_id=1, replica_groups=mesh['hot'=4,'dom'=32] {'dom'}, use_global_device_ids=true, to_apply=%region_18.19 | all-reduce | flops 8 | bytes 64 | tf_op jit(solution)/shard_map/psum | solution.py:127
  585.6 2.8 multiply_reduce_fusion.7
  588.4 62.7 %psum.120 = f32[8]{0:T(128)S(1)} all-reduce(f32[8]{0:T(128)S(1)} %get-tuple-element.173), channel_id=1, replica_groups=mesh['hot'=4,'dom'=32] {'dom'}, use_global_device_ids=true, to_apply=%region_20.21 | all-reduce | flops 8 | bytes 64 | tf_op jit(solution)/shard_map/psum | solution.py:72
  656.0 3.6 collective-permute-start.11
  660.6 5.5 multiply_reduce_fusion.6
  666.0 67.1 %psum.121 = f32[8]{0:T(128)S(1)} all-reduce(f32[8]{0:T(128)S(1)} %get-tuple-element.171), channel_id=1, replica_groups=mesh['hot'=4,'dom'=32] {'dom'}, use_global_device_ids=true, to_apply=%region_22.23 | all-reduce | flops 8 | bytes 64 | tf_op jit(solution)/shard_map/psum | solution.py:127
  733.1 2.8 multiply_reduce_fusion.5
  735.9 62.7 %psum.122 = f32[8]{0:T(128)S(1)} all-reduce(f32[8]{0:T(128)S(1)} %get-tuple-element.169), channel_id=1, replica_groups=mesh['hot'=4,'dom'=32] {'dom'}, use_global_device_ids=true, to_apply=%region_24.25 | all-reduce | flops 8 | bytes 64 | tf_op jit(solution)/shard_map/psum | solution.py:72
  803.5 3.2 collective-permute-start.13
  808.1 5.5 multiply_reduce_fusion.4
  813.6 67.1 %psum.123 = f32[8]{0:T(128)S(1)} all-reduce(f32[8]{0:T(128)S(1)} %get-tuple-element.167), channel_id=1, replica_groups=mesh['hot'=4,'dom'=32] {'dom'}, use_global_device_ids=true, to_apply=%region_26.27 | all-reduce | flops 8 | bytes 64 | tf_op jit(solution)/shard_map/psum | solution.py:127
  880.7 2.8 multiply_reduce_fusion.3
  883.5 62.7 %psum.124 = f32[8]{0:T(128)S(1)} all-reduce(f32[8]{0:T(128)S(1)} %get-tuple-element.165), channel_id=1, replica_groups=mesh['hot'=4,'dom'=32] {'dom'}, use_global_device_ids=true, to_apply=%region_28.29 | all-reduce | flops 8 | bytes 64 | tf_op jit(solution)/shard_map/psum | solution.py:72
  951.0 3.4 collective-permute-start.15
  955.5 5.5 multiply_reduce_fusion.2
  961.0 67.1 %psum.125 = f32[8]{0:T(128)S(1)} all-reduce(f32[8]{0:T(128)S(1)} %get-tuple-element.163), channel_id=1, replica_groups=mesh['hot'=4,'dom'=32] {'dom'}, use_global_device_ids=true, to_apply=%region_30.31 | all-reduce | flops 8 | bytes 64 | tf_op jit(solution)/shard_map/psum | solution.py:127
  1028.2 2.8 multiply_reduce_fusion.1
  1031.0 62.7 %psum.126 = f32[8]{0:T(128)S(1)} all-reduce(f32[8]{0:T(128)S(1)} %get-tuple-element.161), channel_id=1, replica_groups=mesh['hot'=4,'dom'=32] {'dom'}, use_global_device_ids=true, to_apply=%region_32.33 | all-reduce | flops 8 | bytes 64 | tf_op jit(solution)/shard_map/psum | solution.py:72
  1093.7 5.2 multiply_add_fusion.1
  1102.0 3.2 collective-permute-start.17
  1106.6 4.2 multiply_reduce_fusion
  1110.8 67.1 %psum.127 = f32[8]{0:T(128)S(1)} all-reduce(f32[8]{0:T(128)S(1)} %multiply_reduce_fusion), channel_id=1, replica_groups=mesh['hot'=4,'dom'=32] {'dom'}, use_global_device_ids=true, to_apply=%region_34.35 | all-reduce | flops 8 | bytes 64 | tf_op jit(solution)/shard_map/psum | solution.py:127
  1182.6 3.6 collective-permute-done.19
  1186.2 5.1 collective-permute-done.20
  1191.9 3.0 collective-permute-done.21
  1195.6 4.5 collective-permute-done.22
  1200.3 10.0 all-reduce.36
  (334 shorter events, 95.7 us)
Async XLA Ops:
  42.1 17.7 %collective-permute-start = (f32[8,1,4096]{2,1,0:T(1,128)S(1)}, f32[8,1,4096]{2,1,0:T(1,128)S(1)}, u32[]{:S(2)}, u32[]{:S(2)}) collective-permute-start(f32[8,1,4096]{2,1,0:T(1,128)S(1)} %get-tuple-element.256), channel_id=1, source_target_pairs={{1,0},{2,1},{3,2},{4,3},{5,4},{6,5},{7,6},{8,7},{9,8},{10,9},{11,1... | collective-permute-start | bytes 393224 | tf_op jit(solution)/shard_map/ppermute | solution.py:21
  43.4 16.4 %collective-permute-start.1 = (f32[8,1,4096]{2,1,0:T(1,128)S(1)}, f32[8,1,4096]{2,1,0:T(1,128)S(1)}, u32[]{:S(2)}, u32[]{:S(2)}) collective-permute-start(f32[8,1,4096]{2,1,0:T(1,128)S(1)} %get-tuple-element.257), channel_id=1, source_target_pairs={{0,1},{1,2},{2,3},{3,4},{4,5},{5,6},{6,7},{7,8},{8,9},{9,10},{10,1... | collective-permute-start | bytes 393224 | tf_op jit(solution)/shard_map/ppermute | solution.py:20
  46.8 12.8 %copy-start.43 = (s32[8]{0:T(128)S(1)}, s32[8]{0:T(128)}, u32[]{:S(2)}) copy-start(s32[8]{0:T(128)} %param.13) | copy-start | bytes 100
  61.0 83.3 %copy-start.30 = (f32[8,1,2,4096]{3,2,0,1:T(2,128)}, f32[8,1,2,4096]{3,2,0,1:T(2,128)S(1)}, u32[]{:S(2)}) copy-start(f32[8,1,2,4096]{3,2,0,1:T(2,128)S(1)} %get-tuple-element.195) | copy-start | bytes 786436
  61.4 9.6 copy-start.31
  61.4 9.6 copy-start.32
  65.1 5.9 collective-permute-start.2
  66.4 4.6 collective-permute-start.3
  70.9 442.1 %copy-start.14 = (f32[8,2,4096]{2,1,0:T(2,128)}, f32[8,2,4096]{2,1,0:T(2,128)S(1)}, u32[]{:S(2)}) copy-start(f32[8,2,4096]{2,1,0:T(2,128)S(1)} %get-tuple-element.192) | copy-start | bytes 786436
  70.9 442.1 %copy-start.19 = (f32[8,2,4096]{2,1,0:T(2,128)}, f32[8,2,4096]{2,1,0:T(2,128)S(1)}, u32[]{:S(2)}) copy-start(f32[8,2,4096]{2,1,0:T(2,128)S(1)} %get-tuple-element.193) | copy-start | bytes 786436
  71.0 442.1 %copy-start.24 = (f32[8,2,4096]{2,1,0:T(2,128)}, f32[8,2,4096]{2,1,0:T(2,128)S(1)}, u32[]{:S(2)}) copy-start(f32[8,2,4096]{2,1,0:T(2,128)S(1)} %get-tuple-element.194) | copy-start | bytes 786436
  71.0 589.5 %copy-start.2 = (f32[8,2,4096]{2,1,0:T(2,128)}, f32[8,2,4096]{2,1,0:T(2,128)S(1)}, u32[]{:S(2)}) copy-start(f32[8,2,4096]{2,1,0:T(2,128)S(1)} %get-tuple-element.189) | copy-start | bytes 786436
  71.0 589.5 %copy-start.6 = (f32[8,2,4096]{2,1,0:T(2,128)}, f32[8,2,4096]{2,1,0:T(2,128)S(1)}, u32[]{:S(2)}) copy-start(f32[8,2,4096]{2,1,0:T(2,128)S(1)} %get-tuple-element.190) | copy-start | bytes 786436
  71.0 589.5 %copy-start.10 = (f32[8,2,4096]{2,1,0:T(2,128)}, f32[8,2,4096]{2,1,0:T(2,128)S(1)}, u32[]{:S(2)}) copy-start(f32[8,2,4096]{2,1,0:T(2,128)S(1)} %get-tuple-element.191) | copy-start | bytes 786436
  146.3 209.7 %copy-start.29 = (f32[8,3,2,4096]{3,2,0,1:T(2,128)}, f32[8,3,2,4096]{3,2,0,1:T(2,128)S(1)}, u32[]{:S(2)}) copy-start(f32[8,3,2,4096]{3,2,0,1:T(2,128)S(1)} %get-tuple-element.186) | copy-start | bytes 2359300
  212.9 5.3 collective-permute-start.4
  214.2 4.4 collective-permute-start.5
  360.3 5.5 collective-permute-start.6
  361.6 4.4 collective-permute-start.7
  366.0 72.5 %copy-start.33 = (f32[8,3,2,4096]{3,2,0,1:T(2,128)S(1)}, f32[8,3,2,4096]{3,2,0,1:T(2,128)}, u32[]{:S(2)}) copy-start(f32[8,3,2,4096]{3,2,0,1:T(2,128)} %get-tuple-element.182) | copy-start | bytes 2359300
  507.3 5.3 collective-permute-start.8
  508.6 4.4 collective-permute-start.9
  654.6 5.8 collective-permute-start.10
  655.9 4.6 copy-start.15
  655.9 4.6 copy-start.20
  656.0 4.6 copy-start.25
  656.0 4.5 collective-permute-start.11
  802.2 5.5 collective-permute-start.12
  803.5 4.6 copy-start.3
  803.5 4.6 copy-start.7
  803.5 4.5 collective-permute-start.13
  947.8 7.6 copy-start
  949.6 5.6 collective-permute-start.14
  950.9 4.6 copy-start.4
  950.9 4.6 copy-start.8
  951.0 4.5 collective-permute-start.15
  1098.9 7.6 copy-start.1
  1100.7 5.5 collective-permute-start.16
  1102.0 4.6 copy-start.5
  1102.0 4.6 copy-start.9
  1102.0 4.5 collective-permute-start.17
  1106.6 71.4 %copy-start.34 = (f32[8,3,2,4096]{3,2,0,1:T(2,128)S(1)}, f32[8,3,2,4096]{3,2,0,1:T(2,128)}, u32[]{:S(2)}) copy-start(f32[8,3,2,4096]{3,2,0,1:T(2,128)} %get-tuple-element.201) | copy-start | bytes 2359300
  1179.9 11.4 copy-start.44
  1181.3 1.2 collective-permute-start.18
  1182.6 3.6 collective-permute-start.19
  1186.2 5.1 collective-permute-start.20
  1191.3 3.6 collective-permute-start.21
  1194.9 5.1 collective-permute-start.22
  (20 other events, 64.7 us)
